TPU v7x, 32 devices: a whole 2x2x4 slice. The times are simulated.
32 devices in a mesh: groups: 2 (over y), tm: 4 (over x, core), width: 4 (over z).
Axes of the slice: x: 2, y: 2, z: 4, core: 2. Of those that a mesh axis runs over, the one named last changes fastest.
Arguments:
- video: bfloat16 [32, 12, 48, 256], P(('groups', 'tm'), None, 'width'), parts along dimension 0, may hold values from -6 to 6
- conv_w: bfloat16 [2, 3, 3, 256, 256], replicated, may hold values from -0.125 to 0.125
- depth_k: float32 [2, 16, 256], replicated, may hold values from -1.5 to 1.5
- proj_w: bfloat16 [2, 256, 256], replicated, may hold values from -0.375 to 0.375
Outputs:
- result: bfloat16 [32, 12, 48, 256], P(('groups', 'tm'), None, 'width'), parts along dimension 0
There are 2 independent parts, one for each index of `groups`. A program takes and returns all parts, laid end to end along the dimension named above; an argument that names none is the same for every part. Nothing has to cross between parts.
All inputs are finite; a program needn't handle non-finite values.
Results may differ from a plain program's by a relative error of at most 0.0058.
Values may be sent and summed in bfloat16 or wider, within the bound.
No kernel may reach another device: no remote copies, remote signals or barrier semaphores. Data moves between devices by JAX's collectives and lax.ppermute only.
A program may use at most 64 MiB of HBM per device.

v0:
```python
from functools import partial
import jax
import jax.numpy as jnp
from jax import lax
from jax.sharding import PartitionSpec as P

BLOCKS = 2


def with_halo(shard, sides, width):
    for axis, dim in sides:
        peers, length = (lax.axis_size(axis), shard.shape[dim])
        up = [(i, (i + 1) % peers) for i in range(peers - 1)]
        down = [(j, i) for i, j in up]
        last = lax.slice_in_dim(shard, length - width, length, axis=dim)
        leading = lax.slice_in_dim(shard, 0, width, axis=dim)
        before = lax.ppermute(last, axis, up)
        after = lax.ppermute(leading, axis, down)
        shard = jnp.concatenate([before, shard, after], axis=dim)
    return shard


def spatial(padded, weight):
    frames = padded.shape[0]
    rows = padded.shape[1] - 2
    cols = padded.shape[2] - 2
    chans = padded.shape[3]
    total = jnp.zeros((frames * rows * cols, chans), jnp.float32)
    for dy in range(3):
        for dx in range(3):
            piece = padded[:, dy : dy + rows, dx : dx + cols, :].reshape(-1, chans)
            total = total + jnp.dot(piece, weight[dy, dx], preferred_element_type=jnp.float32)
    return total.reshape(frames, rows, cols, chans)


def toeplitz_table(kernel):
    frames = kernel.shape[0]
    later = jnp.arange(frames, dtype=jnp.int32)[:, None]
    earlier = jnp.arange(frames, dtype=jnp.int32)[None, :]
    offset = (later - earlier) % frames
    return jnp.where((later >= earlier)[:, :, None], kernel[offset], jnp.zeros((), jnp.float32))


def temporal(kernel, proj, hidden):
    chans = hidden.shape[-1]
    table = toeplitz_table(kernel)
    values = hidden.astype(jnp.float32)
    total = jnp.einsum("tsc,sijc->tijc", table, values, precision=lax.Precision.HIGHEST)
    depth = total.astype(jnp.bfloat16)
    mixed = jnp.dot(depth.reshape(-1, chans), proj, preferred_element_type=jnp.float32)
    return mixed.reshape(hidden.shape).astype(jnp.bfloat16)


def add_branch(state, mixed):
    return (state.astype(jnp.float32) + mixed.astype(jnp.float32)).astype(jnp.bfloat16)


def shards(video, conv_w, depth_k, proj_w):
    state = video
    for block in range(BLOCKS):
        extended = with_halo(state, (("width", 2),), 1)
        extended = jnp.pad(extended, ((0, 0), (1, 1), (0, 0), (0, 0)))
        hidden = jax.nn.silu(spatial(extended, conv_w[block])).astype(jnp.bfloat16)
        mixer = partial(temporal, depth_k[block], proj_w[block])
        mixed = mixer(lax.all_to_all(hidden, "tm", split_axis=1, concat_axis=0, tiled=True))
        returned = lax.all_to_all(mixed, "tm", split_axis=0, concat_axis=1, tiled=True)
        state = add_branch(state, returned)
    return state


def solution(mesh):
    return jax.shard_map(
        shards,
        mesh=mesh,
        in_specs=(P(("groups", "tm"), None, "width", None), P(), P(), P()),
        out_specs=P(("groups", "tm"), None, "width", None),
        check_vma=False,
    )
```

profile of v0, /device:TPU:0, one launch (start us, length us, event | category | flops | bytes accessed | tf_op | source)
XLA Modules:
  0.0 109.8 jit_solution(14615664582587126943)
XLA Ops:
  0.8 5.0 %collective-permute-start = (bf16[4,12,1,256]{3,0,2,1:T(4,128)(2,1)S(1)}, bf16[4,12,1,256]{3,0,2,1:T(4,128)(2,1)S(1)}, u32[]{:S(2)}, u32[]{:S(2)}) collective-permute-start(bf16[4,12,1,256]{3,0,2,1:T(4,128)(2,1)S(1)} %get-tuple-element.25), channel_id=1, source_target_pairs={{0,1},{1,2},{2,3},{4,5},{5,6},{6,7},{8,9},{9,10},{10,11},{12,13},{... | collective-permute-start | bytes 73736 | tf_op jit(solution)/shard_map/ppermute | solution.py:17
  5.8 1.4 %collective-permute-start.1 = (bf16[4,12,1,256]{3,0,2,1:T(4,128)(2,1)S(1)}, bf16[4,12,1,256]{3,0,2,1:T(4,128)(2,1)S(1)}, u32[]{:S(2)}, u32[]{:S(2)}) collective-permute-start(bf16[4,12,1,256]{3,0,2,1:T(4,128)(2,1)S(1)} %get-tuple-element.26), channel_id=1, source_target_pairs={{1,0},{2,1},{3,2},{5,4},{6,5},{7,6},{9,8},{10,9},{11,10},{13,12},{... | collective-permute-start | bytes 73736 | tf_op jit(solution)/shard_map/ppermute | solution.py:18
  7.2 2.9 %slice_bitcast_fusion = (bf16[3,3,256,256]{3,2,1,0:T(8,128)(2,1)}, bf16[3,3,256,256]{3,2,1,0:T(8,128)(2,1)S(1)}) fusion(bf16[2,3,3,256,256]{4,3,2,1,0:T(8,128)(2,1)} %param.5), kind=kLoop, calls=%fused_computation.32 | loop fusion | bytes 4718592 | tf_op jit(solution)/shard_map/squeeze | solution.py:63
  22.5 0.9 copy.38
  23.4 3.5 %all-to-all-start = ((bf16[4,12,12,256]{3,0,2,1:T(4,128)(2,1)}), bf16[4,12,12,256]{3,0,2,1:T(4,128)(2,1)S(1)}, u32[]{:S(2)}, u32[]{:S(2)}) async-start(bf16[4,12,12,256]{3,0,2,1:T(4,128)(2,1)} %copy.38), calls=%async_computation | async-start | bytes 589824 | tf_op jit(solution)/shard_map/all_to_all | solution.py:65
  26.9 1.0 gather_fusion
  27.9 2.5 %copy.40 = f32[16,16,256]{1,0,2:T(8,128)} copy(f32[16,16,256]{2,1,0:T(8,128)S(1)} %bitcast.149) | data formatting | bytes 524288 | tf_op jit(solution)/shard_map/gather | solution.py:41
  30.4 2.8 %all-to-all-done = bf16[4,12,12,256]{3,0,2,1:T(4,128)(2,1)S(1)} async-done(((bf16[4,12,12,256]{3,0,2,1:T(4,128)(2,1)}), bf16[4,12,12,256]{3,0,2,1:T(4,128)(2,1)S(1)}, u32[]{:S(2)}, u32[]{:S(2)}) %all-to-all-start) | async-done | bytes 294944 | tf_op jit(solution)/shard_map/all_to_all | solution.py:65
  33.4 2.9 %copy.41 = bf16[16,3,12,256]{0,2,1,3:T(8,128)(2,1)S(1)} copy(bf16[16,3,12,256]{3,0,2,1:T(8,128)(2,1)S(1)} %all_to_all.43) | data formatting | bytes 589824 | tf_op jit(solution)/shard_map/all_to_all | solution.py:65
  36.3 6.9 %convert_bitcast_fusion.1 = bf16[16,3,12,256]{0,2,1,3:T(8,128)(2,1)S(1)} fusion(bf16[16,3,12,256]{0,2,1,3:T(8,128)(2,1)S(1)} %copy.41, f32[16,16,256]{1,0,2:T(8,128)} %copy.40, pred[16,16]{1,0:T(8,128)(4,1)S(1)} %iota_compare_fusion.2), kind=kOutput, calls=%fused_computation.3 | convolution fusion | flops 28524544 | bytes 852224 | tf_op jit(solution)/shard_map/tsc,sijc->tijc/dot_general | solution.py:48
  44.1 9.8 %all_to_all.54 = bf16[16,3,12,256]{3,2,1,0:T(8,128)(2,1)S(1)} all-to-all(bf16[16,3,12,256]{3,2,1,0:T(8,128)(2,1)S(1)} %copy.43), channel_id=1, replica_groups=mesh['groups'=2,'tm'=4,'width'=4] {'tm'}, dimensions={0} | all-to-all | bytes 589824 | tf_op jit(solution)/shard_map/all_to_all | solution.py:66
  55.1 3.9 %collective-permute-start.2 = (bf16[4,12,1,256]{3,0,2,1:T(4,128)(2,1)S(1)}, bf16[4,12,1,256]{3,0,2,1:T(4,128)(2,1)S(1)}, u32[]{:S(2)}, u32[]{:S(2)}) collective-permute-start(bf16[4,12,1,256]{3,0,2,1:T(4,128)(2,1)S(1)} %get-tuple-element.21), channel_id=1, source_target_pairs={{0,1},{1,2},{2,3},{4,5},{5,6},{6,7},{8,9},{9,10},{10,11},{12,13},{... | collective-permute-start | bytes 73736 | tf_op jit(solution)/shard_map/ppermute | solution.py:17
  59.0 1.5 %collective-permute-start.3 = (bf16[4,12,1,256]{3,0,2,1:T(4,128)(2,1)S(1)}, bf16[4,12,1,256]{3,0,2,1:T(4,128)(2,1)S(1)}, u32[]{:S(2)}, u32[]{:S(2)}) collective-permute-start(bf16[4,12,1,256]{3,0,2,1:T(4,128)(2,1)S(1)} %get-tuple-element.22), channel_id=1, source_target_pairs={{1,0},{2,1},{3,2},{5,4},{6,5},{7,6},{9,8},{10,9},{11,10},{13,12},{... | collective-permute-start | bytes 73736 | tf_op jit(solution)/shard_map/ppermute | solution.py:18
  60.7 4.1 %collective-permute-done.3 = bf16[4,12,1,256]{3,0,2,1:T(4,128)(2,1)S(1)} collective-permute-done((bf16[4,12,1,256]{3,0,2,1:T(4,128)(2,1)S(1)}, bf16[4,12,1,256]{3,0,2,1:T(4,128)(2,1)S(1)}, u32[]{:S(2)}, u32[]{:S(2)}) %collective-permute-start.3) | collective-permute-done | bytes 24608 | tf_op jit(solution)/shard_map/ppermute | solution.py:18
  75.4 0.9 copy.54
  76.3 3.5 %all-to-all-start.2 = ((bf16[4,12,12,256]{3,0,2,1:T(4,128)(2,1)}), bf16[4,12,12,256]{3,0,2,1:T(4,128)(2,1)S(1)}, u32[]{:S(2)}, u32[]{:S(2)}) async-start(bf16[4,12,12,256]{3,0,2,1:T(4,128)(2,1)} %copy.54), calls=%async_computation.2 | async-start | bytes 589824 | tf_op jit(solution)/shard_map/all_to_all | solution.py:65
  79.8 1.0 gather_fusion.1
  80.7 2.5 %copy.56 = f32[16,16,256]{1,0,2:T(8,128)} copy(f32[16,16,256]{2,1,0:T(8,128)S(1)} %bitcast.148) | data formatting | bytes 524288 | tf_op jit(solution)/shard_map/gather | solution.py:41
  83.2 2.9 %all-to-all-done.2 = bf16[4,12,12,256]{3,0,2,1:T(4,128)(2,1)S(1)} async-done(((bf16[4,12,12,256]{3,0,2,1:T(4,128)(2,1)}), bf16[4,12,12,256]{3,0,2,1:T(4,128)(2,1)S(1)}, u32[]{:S(2)}, u32[]{:S(2)}) %all-to-all-start.2) | async-done | bytes 294944 | tf_op jit(solution)/shard_map/all_to_all | solution.py:65
  86.2 0.8 all_to_all.48
  87.0 3.8 %copy.57 = bf16[16,3,12,256]{0,2,1,3:T(8,128)(2,1)S(1)} copy(bf16[16,3,12,256]{3,0,2,1:T(8,128)(2,1)} %all_to_all.48) | data formatting | bytes 589824 | tf_op jit(solution)/shard_map/all_to_all | solution.py:65
  90.8 6.9 %convert_bitcast_fusion = bf16[16,3,12,256]{0,2,1,3:T(8,128)(2,1)S(1)} fusion(bf16[16,3,12,256]{0,2,1,3:T(8,128)(2,1)S(1)} %copy.57, f32[16,16,256]{1,0,2:T(8,128)} %copy.56, pred[16,16]{1,0:T(8,128)(4,1)S(1)} %iota_compare_fusion.2), kind=kOutput, calls=%fused_computation.2 | convolution fusion | flops 28524544 | bytes 852224 | tf_op jit(solution)/shard_map/tsc,sijc->tijc/dot_general | solution.py:48
  98.6 9.8 %all_to_all.55 = bf16[16,3,12,256]{3,2,1,0:T(8,128)(2,1)S(1)} all-to-all(bf16[16,3,12,256]{3,2,1,0:T(8,128)(2,1)S(1)} %copy.59), channel_id=1, replica_groups=mesh['groups'=2,'tm'=4,'width'=4] {'tm'}, dimensions={0} | all-to-all | bytes 589824 | tf_op jit(solution)/shard_map/all_to_all | solution.py:66
  108.9 0.9 fusion.19
  (120 shorter events, 27.2 us)
Async XLA Ops:
  0.8 10.2 %collective-permute-start = (bf16[4,12,1,256]{3,0,2,1:T(4,128)(2,1)S(1)}, bf16[4,12,1,256]{3,0,2,1:T(4,128)(2,1)S(1)}, u32[]{:S(2)}, u32[]{:S(2)}) collective-permute-start(bf16[4,12,1,256]{3,0,2,1:T(4,128)(2,1)S(1)} %get-tuple-element.25), channel_id=1, source_target_pairs={{0,1},{1,2},{2,3},{4,5},{5,6},{6,7},{8,9},{9,10},{10,11},{12,13},{... | collective-permute-start | bytes 73736 | tf_op jit(solution)/shard_map/ppermute | solution.py:17
  5.7 4.3 %copy-start.14 = (f32[2,16,256]{2,1,0:T(8,128)S(1)}, f32[2,16,256]{2,1,0:T(8,128)}, u32[]{:S(2)}) copy-start(f32[2,16,256]{2,1,0:T(8,128)} %param.6) | copy-start | bytes 98308
  5.8 4.3 %copy-start = (bf16[4,12,12,256]{3,0,2,1:T(4,128)(2,1)S(1)}, bf16[4,12,12,256]{3,0,2,1:T(4,128)(2,1)}, u32[]{:S(2)}) copy-start(bf16[4,12,12,256]{3,0,2,1:T(4,128)(2,1)} %param.4) | copy-start | bytes 884740
  5.8 5.9 %collective-permute-start.1 = (bf16[4,12,1,256]{3,0,2,1:T(4,128)(2,1)S(1)}, bf16[4,12,1,256]{3,0,2,1:T(4,128)(2,1)S(1)}, u32[]{:S(2)}, u32[]{:S(2)}) collective-permute-start(bf16[4,12,1,256]{3,0,2,1:T(4,128)(2,1)S(1)} %get-tuple-element.26), channel_id=1, source_target_pairs={{1,0},{2,1},{3,2},{5,4},{6,5},{7,6},{9,8},{10,9},{11,10},{13,12},{... | collective-permute-start | bytes 73736 | tf_op jit(solution)/shard_map/ppermute | solution.py:18
  16.1 1.0 copy-start.4
  16.2 1.1 %copy-start.5 = (bf16[576,256]{1,0:T(8,128)(2,1)S(1)}, bf16[576,256]{1,0:T(8,128)(2,1)}, u32[]{:S(2)}) copy-start(bf16[576,256]{1,0:T(8,128)(2,1)} %reshape.147) | copy-start | bytes 884740
  17.6 1.0 copy-start.8
  18.6 1.0 copy-start.3
  19.5 1.0 copy-start.6
  21.0 1.0 copy-start.12
  23.4 9.8 %all-to-all-start = ((bf16[4,12,12,256]{3,0,2,1:T(4,128)(2,1)}), bf16[4,12,12,256]{3,0,2,1:T(4,128)(2,1)S(1)}, u32[]{:S(2)}, u32[]{:S(2)}) async-start(bf16[4,12,12,256]{3,0,2,1:T(4,128)(2,1)} %copy.38), calls=%async_computation | async-start | bytes 589824 | tf_op jit(solution)/shard_map/all_to_all | solution.py:65
  36.3 6.9 %copy-start.15 = (bf16[2,256,256]{2,1,0:T(8,128)(2,1)S(1)}, bf16[2,256,256]{2,1,0:T(8,128)(2,1)}, u32[]{:S(2)}) copy-start(bf16[2,256,256]{2,1,0:T(8,128)(2,1)} %param.7) | copy-start | bytes 786436
  53.9 1.0 copy-start.1
  55.1 5.6 %collective-permute-start.2 = (bf16[4,12,1,256]{3,0,2,1:T(4,128)(2,1)S(1)}, bf16[4,12,1,256]{3,0,2,1:T(4,128)(2,1)S(1)}, u32[]{:S(2)}, u32[]{:S(2)}) collective-permute-start(bf16[4,12,1,256]{3,0,2,1:T(4,128)(2,1)S(1)} %get-tuple-element.21), channel_id=1, source_target_pairs={{0,1},{1,2},{2,3},{4,5},{5,6},{6,7},{8,9},{9,10},{10,11},{12,13},{... | collective-permute-start | bytes 73736 | tf_op jit(solution)/shard_map/ppermute | solution.py:17
  59.0 5.7 %collective-permute-start.3 = (bf16[4,12,1,256]{3,0,2,1:T(4,128)(2,1)S(1)}, bf16[4,12,1,256]{3,0,2,1:T(4,128)(2,1)S(1)}, u32[]{:S(2)}, u32[]{:S(2)}) collective-permute-start(bf16[4,12,1,256]{3,0,2,1:T(4,128)(2,1)S(1)} %get-tuple-element.22), channel_id=1, source_target_pairs={{1,0},{2,1},{3,2},{5,4},{6,5},{7,6},{9,8},{10,9},{11,10},{13,12},{... | collective-permute-start | bytes 73736 | tf_op jit(solution)/shard_map/ppermute | solution.py:18
  68.6 1.6 %copy-start.2 = (bf16[3,3,256,256]{3,2,1,0:T(8,128)(2,1)S(1)}, bf16[3,3,256,256]{3,2,1,0:T(8,128)(2,1)}, u32[]{:S(2)}) copy-start(bf16[3,3,256,256]{3,2,1,0:T(8,128)(2,1)} %get-tuple-element.5) | copy-start | bytes 3538948
  69.4 1.1 copy-start.10
  70.2 1.0 copy-start.13
  71.9 1.0 copy-start.7
  72.9 1.0 copy-start.9
  73.9 1.0 copy-start.11
  76.3 9.8 %all-to-all-start.2 = ((bf16[4,12,12,256]{3,0,2,1:T(4,128)(2,1)}), bf16[4,12,12,256]{3,0,2,1:T(4,128)(2,1)S(1)}, u32[]{:S(2)}, u32[]{:S(2)}) async-start(bf16[4,12,12,256]{3,0,2,1:T(4,128)(2,1)} %copy.54), calls=%async_computation.2 | async-start | bytes 589824 | tf_op jit(solution)/shard_map/all_to_all | solution.py:65
  90.8 6.9 %copy-start.16 = (bf16[2,256,256]{2,1,0:T(8,128)(2,1)S(1)}, bf16[2,256,256]{2,1,0:T(8,128)(2,1)}, u32[]{:S(2)}) copy-start(bf16[2,256,256]{2,1,0:T(8,128)(2,1)} %param.7) | copy-start | bytes 786436
where the time goes:
time: 111 us; the launch traced here: 110 us
  local copies, waits for them, and re-layouts  38.4 us (35%)
  blocking collectives  19.6 us (18%)
  matrix products  19.4 us (17%)
  starting transfers between devices  18.7 us (17%)
  waiting for transfers between devices  10.4 us (9%)
  other arithmetic  2.54 us (2%)
    all_to_all x2, blocking collectives, shards(): lax.all_to_all(mixed, 'tm', split_axis=0, concat_axis=1, tiled=True)  19.6 us
    dot_general x2, matrix products, temporal(): jnp.einsum('tsc,sijc->tijc', table, values, precision=lax.Precision.HIGHEST)  13.7 us
    reshape x18, local copies, waits for them, and re-layouts, spatial(): piece = padded[:, dy:dy + rows, dx:dx + cols, :].reshape(-1, chans)  9.05 us
    ppermute x2, starting transfers between devices, with_halo(): before = lax.ppermute(last, axis, up)  8.9 us
    all_to_all x6, local copies, waits for them, and re-layouts, shards(): lax.all_to_all(hidden, 'tm', split_axis=1, concat_axis=0, tiled=True)  7.8 us
    gather x4, local copies, waits for them, and re-layouts, toeplitz_table(): kernel[offset]  6.91 us
    all_to_all x2, starting transfers between devices, shards(): lax.all_to_all(hidden, 'tm', split_axis=1, concat_axis=0, tiled=True)  6.9 us
    unnamed x35, local copies, waits for them, and re-layouts  6.14 us
  transfers between devices with their start and end apart: 6, of which 4 were waited for; matrix products, arithmetic and copies ran while one was open for 10% of the time, Pallas kernels for 0%

commit v1 on v0

--- a/solution.py
+++ b/solution.py
@@ -5,6 +5,22 @@
 from jax.sharding import PartitionSpec as P
 
 BLOCKS = 2
+
+
+def map_ranges(row_data, d_out, x_part):
+    work_now = row_data.shape
+    far_arr = row_data.reshape(
+        *work_now[:d_out], x_part, work_now[d_out] // x_part, *work_now[d_out + 1 :]
+    )
+    b_now = jnp.moveaxis(far_arr, d_out, 0)
+    return b_now
+
+
+def finish_scenes(x_in, d0):
+    block_out = list(x_in.shape[1:])
+    block_out[d0] *= x_in.shape[0]
+    e_now = jnp.moveaxis(x_in, 0, d0).reshape(block_out)
+    return e_now
 
 
 def with_halo(shard, sides, width):
@@ -63,7 +79,16 @@
         hidden = jax.nn.silu(spatial(extended, conv_w[block])).astype(jnp.bfloat16)
         mixer = partial(temporal, depth_k[block], proj_w[block])
         mixed = mixer(lax.all_to_all(hidden, "tm", split_axis=1, concat_axis=0, tiled=True))
-        returned = lax.all_to_all(mixed, "tm", split_axis=0, concat_axis=1, tiled=True)
+        clean = lax.axis_size("tm")
+        tmp, then = (clean, lax.axis_index("tm"))
+        side_arr = map_ranges(mixed, 0, tmp)
+        so_far_all = [side_arr[then]]
+        for rr in tuple(range(1, tmp)):
+            everything = side_arr[then ^ rr]
+            so_far_all.append(lax.ppermute(everything, "tm", [(no, no ^ rr) for no in range(tmp)]))
+        o_now = jnp.stack(so_far_all)
+        side_arr = o_now[then ^ jnp.arange(tmp)]
+        returned = finish_scenes(side_arr, 1)
         state = add_branch(state, returned)
     return state
 

time: 111 us -> 107 us (0.964)
  blocking collectives: 19.6 us -> 0 us
  waiting for transfers between devices: 10.4 us -> 21 us
  starting transfers between devices: 18.7 us -> 23 us
    all_to_all x2 -> x0, blocking collectives: 19.6 us -> none  [shards(): lax.all_to_all(mixed, 'tm', split_axis=0, concat_axis=1, tiled=True)]
    ppermute x0 -> x6, waiting for transfers between devices: none -> 7.71 us  [shards(): lax.ppermute(everything, 'tm', [(no, no ^ rr) for no in range(tmp)])]
    ppermute x0 -> x6, starting transfers between devices: none -> 3.84 us  [shards(): lax.ppermute(everything, 'tm', [(no, no ^ rr) for no in range(tmp)])]
    all_to_all x2, waiting for transfers between devices: 5.7 us -> 9.16 us  [shards(): lax.all_to_all(hidden, 'tm', split_axis=1, concat_axis=0, tiled=True)]
    gather x0 -> x2, local copies, waits for them, and re-layouts: none -> 1.66 us  [shards(): side_arr = o_now[then ^ jnp.arange(tmp)]]
  transfers between devices with their start and end apart: 6 -> 12, of which waited for: 4 -> 7; matrix products, arithmetic and copies ran while one was open for 10% -> 10% of each run, Pallas kernels for 0% -> 0%
where the time goes in v1:
time: 107 us; the launch traced here: 106 us
  local copies, waits for them, and re-layouts  39 us (36%)
  starting transfers between devices  23 us (21%)
  waiting for transfers between devices  21 us (20%)
  matrix products  19.4 us (18%)
  other arithmetic  2.74 us (3%)
    dot_general x2, matrix products, temporal(): jnp.einsum('tsc,sijc->tijc', table, values, precision=lax.Precision.HIGHEST)  13.7 us
    ppermute x2, starting transfers between devices, with_halo(): before = lax.ppermute(last, axis, up)  9.51 us
    all_to_all x2, waiting for transfers between devices, shards(): lax.all_to_all(hidden, 'tm', split_axis=1, concat_axis=0, tiled=True)  9.16 us
    reshape x18, local copies, waits for them, and re-layouts, spatial(): piece = padded[:, dy:dy + rows, dx:dx + cols, :].reshape(-1, chans)  9.11 us
    all_to_all x6, local copies, waits for them, and re-layouts, shards(): lax.all_to_all(hidden, 'tm', split_axis=1, concat_axis=0, tiled=True)  7.8 us
    ppermute x6, waiting for transfers between devices, shards(): lax.ppermute(everything, 'tm', [(no, no ^ rr) for no in range(tmp)])  7.71 us
    gather x4, local copies, waits for them, and re-layouts, toeplitz_table(): kernel[offset]  6.9 us
    all_to_all x2, starting transfers between devices, shards(): lax.all_to_all(hidden, 'tm', split_axis=1, concat_axis=0, tiled=True)  6.9 us
  transfers between devices with their start and end apart: 12, of which 7 were waited for; matrix products, arithmetic and copies ran while one was open for 10% of the time, Pallas kernels for 0%

profile of v1, /device:TPU:0, one launch (start us, length us, event | category | flops | bytes accessed | tf_op | source)
XLA Modules:
  0.0 105.9 jit_solution(15507798509027428585)
XLA Ops:
  0.8 5.0 %collective-permute-start = (bf16[4,12,1,256]{3,0,2,1:T(4,128)(2,1)S(1)}, bf16[4,12,1,256]{3,0,2,1:T(4,128)(2,1)S(1)}, u32[]{:S(2)}, u32[]{:S(2)}) collective-permute-start(bf16[4,12,1,256]{3,0,2,1:T(4,128)(2,1)S(1)} %get-tuple-element.33), channel_id=1, source_target_pairs={{0,1},{1,2},{2,3},{4,5},{5,6},{6,7},{8,9},{9,10},{10,11},{12,13},{... | collective-permute-start | bytes 73736 | tf_op jit(solution)/shard_map/ppermute | solution.py:33
  5.7 1.3 %collective-permute-start.1 = (bf16[4,12,1,256]{3,0,2,1:T(4,128)(2,1)S(1)}, bf16[4,12,1,256]{3,0,2,1:T(4,128)(2,1)S(1)}, u32[]{:S(2)}, u32[]{:S(2)}) collective-permute-start(bf16[4,12,1,256]{3,0,2,1:T(4,128)(2,1)S(1)} %get-tuple-element.34), channel_id=1, source_target_pairs={{1,0},{2,1},{3,2},{5,4},{6,5},{7,6},{9,8},{10,9},{11,10},{13,12},{... | collective-permute-start | bytes 73736 | tf_op jit(solution)/shard_map/ppermute | solution.py:34
  7.1 2.9 %slice_bitcast_fusion = (bf16[3,3,256,256]{3,2,1,0:T(8,128)(2,1)}, bf16[3,3,256,256]{3,2,1,0:T(8,128)(2,1)S(1)}) fusion(bf16[2,3,3,256,256]{4,3,2,1,0:T(8,128)(2,1)} %param.5), kind=kLoop, calls=%fused_computation.34 | loop fusion | bytes 4718592 | tf_op jit(solution)/shard_map/squeeze | solution.py:79
  10.9 1.0 gather_fusion
  11.9 2.5 %copy.36 = f32[16,16,256]{1,0,2:T(8,128)} copy(f32[16,16,256]{2,1,0:T(8,128)S(1)} %bitcast.171) | data formatting | bytes 524288 | tf_op jit(solution)/shard_map/gather | solution.py:57
  25.2 0.9 copy.34
  26.2 3.5 %all-to-all-start = ((bf16[4,12,12,256]{3,0,2,1:T(4,128)(2,1)}), bf16[4,12,12,256]{3,0,2,1:T(4,128)(2,1)S(1)}, u32[]{:S(2)}, u32[]{:S(2)}) async-start(bf16[4,12,12,256]{3,0,2,1:T(4,128)(2,1)} %copy.34), calls=%async_computation | async-start | bytes 589824 | tf_op jit(solution)/shard_map/all_to_all | solution.py:81
  29.7 6.3 %all-to-all-done = bf16[4,12,12,256]{3,0,2,1:T(4,128)(2,1)S(1)} async-done(((bf16[4,12,12,256]{3,0,2,1:T(4,128)(2,1)}), bf16[4,12,12,256]{3,0,2,1:T(4,128)(2,1)S(1)}, u32[]{:S(2)}, u32[]{:S(2)}) %all-to-all-start) | async-done | bytes 294944 | tf_op jit(solution)/shard_map/all_to_all | solution.py:81
  36.2 2.9 %copy.37 = bf16[16,3,12,256]{0,2,1,3:T(8,128)(2,1)S(1)} copy(bf16[16,3,12,256]{3,0,2,1:T(8,128)(2,1)S(1)} %all_to_all.29) | data formatting | bytes 589824 | tf_op jit(solution)/shard_map/all_to_all | solution.py:81
  39.1 6.9 %convert_bitcast_fusion.1 = bf16[16,3,12,256]{0,2,1,3:T(8,128)(2,1)S(1)} fusion(bf16[16,3,12,256]{0,2,1,3:T(8,128)(2,1)S(1)} %copy.37, f32[16,16,256]{1,0,2:T(8,128)} %copy.36, pred[16,16]{1,0:T(8,128)(4,1)S(1)} %iota_compare_fusion.2), kind=kOutput, calls=%fused_computation.5 | convolution fusion | flops 28524544 | bytes 852224 | tf_op jit(solution)/shard_map/tsc,sijc->tijc/dot_general | solution.py:64
  47.5 1.4 %collective-permute-start.4 = (bf16[4,3,12,256]{3,0,2,1:T(4,128)(2,1)S(1)}, bf16[4,3,12,256]{3,0,2,1:T(4,128)(2,1)S(1)}, u32[]{:S(2)}, u32[]{:S(2)}) collective-permute-start(bf16[4,3,12,256]{3,0,2,1:T(4,128)(2,1)S(1)} %get-tuple-element.28), channel_id=1, source_target_pairs={{0,12},{4,8},{8,4},{12,0},{1,13},{5,9},{9,5},{13,1},{2,14},{6,10},... | collective-permute-start | bytes 221192 | tf_op jit(solution)/shard_map/ppermute | solution.py:88
  48.9 3.3 %collective-permute-done.3 = bf16[4,3,12,256]{3,0,2,1:T(4,128)(2,1)S(1)} collective-permute-done((bf16[4,3,12,256]{3,0,2,1:T(4,128)(2,1)S(1)}, bf16[4,3,12,256]{3,0,2,1:T(4,128)(2,1)S(1)}, u32[]{:S(2)}, u32[]{:S(2)}) %collective-permute-start.3) | collective-permute-done | bytes 73760 | tf_op jit(solution)/shard_map/ppermute | solution.py:88
  54.0 4.5 %collective-permute-start.5 = (bf16[4,12,1,256]{3,0,2,1:T(4,128)(2,1)S(1)}, bf16[4,12,1,256]{3,0,2,1:T(4,128)(2,1)S(1)}, u32[]{:S(2)}, u32[]{:S(2)}) collective-permute-start(bf16[4,12,1,256]{3,0,2,1:T(4,128)(2,1)S(1)} %get-tuple-element.25), channel_id=1, source_target_pairs={{0,1},{1,2},{2,3},{4,5},{5,6},{6,7},{8,9},{9,10},{10,11},{12,13},{... | collective-permute-start | bytes 73736 | tf_op jit(solution)/shard_map/ppermute | solution.py:33
  58.6 1.5 %collective-permute-start.6 = (bf16[4,12,1,256]{3,0,2,1:T(4,128)(2,1)S(1)}, bf16[4,12,1,256]{3,0,2,1:T(4,128)(2,1)S(1)}, u32[]{:S(2)}, u32[]{:S(2)}) collective-permute-start(bf16[4,12,1,256]{3,0,2,1:T(4,128)(2,1)S(1)} %get-tuple-element.26), channel_id=1, source_target_pairs={{1,0},{2,1},{3,2},{5,4},{6,5},{7,6},{9,8},{10,9},{11,10},{13,12},{... | collective-permute-start | bytes 73736 | tf_op jit(solution)/shard_map/ppermute | solution.py:34
  60.2 4.1 %collective-permute-done.6 = bf16[4,12,1,256]{3,0,2,1:T(4,128)(2,1)S(1)} collective-permute-done((bf16[4,12,1,256]{3,0,2,1:T(4,128)(2,1)S(1)}, bf16[4,12,1,256]{3,0,2,1:T(4,128)(2,1)S(1)}, u32[]{:S(2)}, u32[]{:S(2)}) %collective-permute-start.6) | collective-permute-done | bytes 24608 | tf_op jit(solution)/shard_map/ppermute | solution.py:34
  74.9 0.9 copy.48
  75.8 3.5 %all-to-all-start.1 = ((bf16[4,12,12,256]{3,0,2,1:T(4,128)(2,1)}), bf16[4,12,12,256]{3,0,2,1:T(4,128)(2,1)S(1)}, u32[]{:S(2)}, u32[]{:S(2)}) async-start(bf16[4,12,12,256]{3,0,2,1:T(4,128)(2,1)} %copy.48), calls=%async_computation.1 | async-start | bytes 589824 | tf_op jit(solution)/shard_map/all_to_all | solution.py:81
  79.3 1.0 gather_fusion.2
  80.3 2.5 %copy.50 = f32[16,16,256]{1,0,2:T(8,128)} copy(f32[16,16,256]{2,1,0:T(8,128)S(1)} %bitcast.170) | data formatting | bytes 524288 | tf_op jit(solution)/shard_map/gather | solution.py:57
  82.8 2.9 %all-to-all-done.1 = bf16[4,12,12,256]{3,0,2,1:T(4,128)(2,1)S(1)} async-done(((bf16[4,12,12,256]{3,0,2,1:T(4,128)(2,1)}), bf16[4,12,12,256]{3,0,2,1:T(4,128)(2,1)S(1)}, u32[]{:S(2)}, u32[]{:S(2)}) %all-to-all-start.1) | async-done | bytes 294944 | tf_op jit(solution)/shard_map/all_to_all | solution.py:81
  86.5 3.8 %copy.51 = bf16[16,3,12,256]{0,2,1,3:T(8,128)(2,1)S(1)} copy(bf16[16,3,12,256]{3,0,2,1:T(8,128)(2,1)} %all_to_all.33) | data formatting | bytes 589824 | tf_op jit(solution)/shard_map/all_to_all | solution.py:81
  90.3 6.9 %convert_bitcast_fusion = bf16[16,3,12,256]{0,2,1,3:T(8,128)(2,1)S(1)} fusion(bf16[16,3,12,256]{0,2,1,3:T(8,128)(2,1)S(1)} %copy.51, f32[16,16,256]{1,0,2:T(8,128)} %copy.50, pred[16,16]{1,0:T(8,128)(4,1)S(1)} %iota_compare_fusion.2), kind=kOutput, calls=%fused_computation.4 | convolution fusion | flops 28524544 | bytes 852224 | tf_op jit(solution)/shard_map/tsc,sijc->tijc/dot_general | solution.py:64
  98.7 1.4 %collective-permute-start.9 = (bf16[4,3,12,256]{3,0,2,1:T(4,128)(2,1)S(1)}, bf16[4,3,12,256]{3,0,2,1:T(4,128)(2,1)S(1)}, u32[]{:S(2)}, u32[]{:S(2)}) collective-permute-start(bf16[4,3,12,256]{3,0,2,1:T(4,128)(2,1)S(1)} %get-tuple-element.20), channel_id=1, source_target_pairs={{0,12},{4,8},{8,4},{12,0},{1,13},{5,9},{9,5},{13,1},{2,14},{6,10},... | collective-permute-start | bytes 221192 | tf_op jit(solution)/shard_map/ppermute | solution.py:88
  100.1 3.4 %collective-permute-done.8 = bf16[4,3,12,256]{3,0,2,1:T(4,128)(2,1)S(1)} collective-permute-done((bf16[4,3,12,256]{3,0,2,1:T(4,128)(2,1)S(1)}, bf16[4,3,12,256]{3,0,2,1:T(4,128)(2,1)S(1)}, u32[]{:S(2)}, u32[]{:S(2)}) %collective-permute-start.8) | collective-permute-done | bytes 73760 | tf_op jit(solution)/shard_map/ppermute | solution.py:88
  (134 shorter events, 31.1 us)
Async XLA Ops:
  0.8 13.6 %collective-permute-start = (bf16[4,12,1,256]{3,0,2,1:T(4,128)(2,1)S(1)}, bf16[4,12,1,256]{3,0,2,1:T(4,128)(2,1)S(1)}, u32[]{:S(2)}, u32[]{:S(2)}) collective-permute-start(bf16[4,12,1,256]{3,0,2,1:T(4,128)(2,1)S(1)} %get-tuple-element.33), channel_id=1, source_target_pairs={{0,1},{1,2},{2,3},{4,5},{5,6},{6,7},{8,9},{9,10},{10,11},{12,13},{... | collective-permute-start | bytes 73736 | tf_op jit(solution)/shard_map/ppermute | solution.py:33
  5.7 8.6 %collective-permute-start.1 = (bf16[4,12,1,256]{3,0,2,1:T(4,128)(2,1)S(1)}, bf16[4,12,1,256]{3,0,2,1:T(4,128)(2,1)S(1)}, u32[]{:S(2)}, u32[]{:S(2)}) collective-permute-start(bf16[4,12,1,256]{3,0,2,1:T(4,128)(2,1)S(1)} %get-tuple-element.34), channel_id=1, source_target_pairs={{1,0},{2,1},{3,2},{5,4},{6,5},{7,6},{9,8},{10,9},{11,10},{13,12},{... | collective-permute-start | bytes 73736 | tf_op jit(solution)/shard_map/ppermute | solution.py:34
  7.1 2.9 %copy-start.14 = (f32[2,16,256]{2,1,0:T(8,128)S(1)}, f32[2,16,256]{2,1,0:T(8,128)}, u32[]{:S(2)}) copy-start(f32[2,16,256]{2,1,0:T(8,128)} %param.6) | copy-start | bytes 98308
  7.1 3.0 %copy-start = (bf16[4,12,12,256]{3,0,2,1:T(4,128)(2,1)S(1)}, bf16[4,12,12,256]{3,0,2,1:T(4,128)(2,1)}, u32[]{:S(2)}) copy-start(bf16[4,12,12,256]{3,0,2,1:T(4,128)(2,1)} %param.4) | copy-start | bytes 884740
  18.9 1.0 copy-start.4
  19.0 1.1 %copy-start.5 = (bf16[576,256]{1,0:T(8,128)(2,1)S(1)}, bf16[576,256]{1,0:T(8,128)(2,1)}, u32[]{:S(2)}) copy-start(bf16[576,256]{1,0:T(8,128)(2,1)} %reshape.167) | copy-start | bytes 884740
  23.8 1.0 copy-start.12
  26.2 9.8 %all-to-all-start = ((bf16[4,12,12,256]{3,0,2,1:T(4,128)(2,1)}), bf16[4,12,12,256]{3,0,2,1:T(4,128)(2,1)S(1)}, u32[]{:S(2)}, u32[]{:S(2)}) async-start(bf16[4,12,12,256]{3,0,2,1:T(4,128)(2,1)} %copy.34), calls=%async_computation | async-start | bytes 589824 | tf_op jit(solution)/shard_map/all_to_all | solution.py:81
  39.1 6.9 %copy-start.15 = (bf16[2,256,256]{2,1,0:T(8,128)(2,1)S(1)}, bf16[2,256,256]{2,1,0:T(8,128)(2,1)}, u32[]{:S(2)}) copy-start(bf16[2,256,256]{2,1,0:T(8,128)(2,1)} %param.7) | copy-start | bytes 786436
  46.8 7.1 %copy-start.1 = (bf16[4,12,12,256]{3,0,2,1:T(4,128)(2,1)S(1)}, bf16[4,12,12,256]{3,0,2,1:T(4,128)(2,1)}, u32[]{:S(2)}) copy-start(bf16[4,12,12,256]{3,0,2,1:T(4,128)(2,1)} %param.4) | copy-start | bytes 884740
  47.0 1.9 %collective-permute-start.2 = (bf16[4,3,12,256]{3,0,2,1:T(4,128)(2,1)S(1)}, bf16[4,3,12,256]{3,0,2,1:T(4,128)(2,1)S(1)}, u32[]{:S(2)}, u32[]{:S(2)}) collective-permute-start(bf16[4,3,12,256]{3,0,2,1:T(4,128)(2,1)S(1)} %get-tuple-element.30), channel_id=1, source_target_pairs={{0,4},{4,0},{8,12},{12,8},{1,5},{5,1},{9,13},{13,9},{2,6},{6,2},{1... | collective-permute-start | bytes 221192 | tf_op jit(solution)/shard_map/ppermute | solution.py:88
  47.1 5.2 %collective-permute-start.3 = (bf16[4,3,12,256]{3,0,2,1:T(4,128)(2,1)S(1)}, bf16[4,3,12,256]{3,0,2,1:T(4,128)(2,1)S(1)}, u32[]{:S(2)}, u32[]{:S(2)}) collective-permute-start(bf16[4,3,12,256]{3,0,2,1:T(4,128)(2,1)S(1)} %get-tuple-element.29), channel_id=1, source_target_pairs={{0,8},{4,12},{8,0},{12,4},{1,9},{5,13},{9,1},{13,5},{2,10},{6,14},... | collective-permute-start | bytes 221192 | tf_op jit(solution)/shard_map/ppermute | solution.py:88
  47.5 5.3 %collective-permute-start.4 = (bf16[4,3,12,256]{3,0,2,1:T(4,128)(2,1)S(1)}, bf16[4,3,12,256]{3,0,2,1:T(4,128)(2,1)S(1)}, u32[]{:S(2)}, u32[]{:S(2)}) collective-permute-start(bf16[4,3,12,256]{3,0,2,1:T(4,128)(2,1)S(1)} %get-tuple-element.28), channel_id=1, source_target_pairs={{0,12},{4,8},{8,4},{12,0},{1,13},{5,9},{9,5},{13,1},{2,14},{6,10},... | collective-permute-start | bytes 221192 | tf_op jit(solution)/shard_map/ppermute | solution.py:88
  54.0 6.2 %collective-permute-start.5 = (bf16[4,12,1,256]{3,0,2,1:T(4,128)(2,1)S(1)}, bf16[4,12,1,256]{3,0,2,1:T(4,128)(2,1)S(1)}, u32[]{:S(2)}, u32[]{:S(2)}) collective-permute-start(bf16[4,12,1,256]{3,0,2,1:T(4,128)(2,1)S(1)} %get-tuple-element.25), channel_id=1, source_target_pairs={{0,1},{1,2},{2,3},{4,5},{5,6},{6,7},{8,9},{9,10},{10,11},{12,13},{... | collective-permute-start | bytes 73736 | tf_op jit(solution)/shard_map/ppermute | solution.py:33
  58.6 5.7 %collective-permute-start.6 = (bf16[4,12,1,256]{3,0,2,1:T(4,128)(2,1)S(1)}, bf16[4,12,1,256]{3,0,2,1:T(4,128)(2,1)S(1)}, u32[]{:S(2)}, u32[]{:S(2)}) collective-permute-start(bf16[4,12,1,256]{3,0,2,1:T(4,128)(2,1)S(1)} %get-tuple-element.26), channel_id=1, source_target_pairs={{1,0},{2,1},{3,2},{5,4},{6,5},{7,6},{9,8},{10,9},{11,10},{13,12},{... | collective-permute-start | bytes 73736 | tf_op jit(solution)/shard_map/ppermute | solution.py:34
  68.1 1.7 %copy-start.2 = (bf16[3,3,256,256]{3,2,1,0:T(8,128)(2,1)S(1)}, bf16[3,3,256,256]{3,2,1,0:T(8,128)(2,1)}, u32[]{:S(2)}) copy-start(bf16[3,3,256,256]{3,2,1,0:T(8,128)(2,1)} %get-tuple-element.5) | copy-start | bytes 3538948
  69.0 1.1 copy-start.10
  69.8 1.0 copy-start.13
  71.5 1.0 copy-start.7
  75.8 9.8 %all-to-all-start.1 = ((bf16[4,12,12,256]{3,0,2,1:T(4,128)(2,1)}), bf16[4,12,12,256]{3,0,2,1:T(4,128)(2,1)S(1)}, u32[]{:S(2)}, u32[]{:S(2)}) async-start(bf16[4,12,12,256]{3,0,2,1:T(4,128)(2,1)} %copy.48), calls=%async_computation.1 | async-start | bytes 589824 | tf_op jit(solution)/shard_map/all_to_all | solution.py:81
  90.3 6.9 %copy-start.16 = (bf16[2,256,256]{2,1,0:T(8,128)(2,1)S(1)}, bf16[2,256,256]{2,1,0:T(8,128)(2,1)}, u32[]{:S(2)}) copy-start(bf16[2,256,256]{2,1,0:T(8,128)(2,1)} %param.7) | copy-start | bytes 786436
  98.2 1.9 %collective-permute-start.7 = (bf16[4,3,12,256]{3,0,2,1:T(4,128)(2,1)S(1)}, bf16[4,3,12,256]{3,0,2,1:T(4,128)(2,1)S(1)}, u32[]{:S(2)}, u32[]{:S(2)}) collective-permute-start(bf16[4,3,12,256]{3,0,2,1:T(4,128)(2,1)S(1)} %get-tuple-element.22), channel_id=1, source_target_pairs={{0,4},{4,0},{8,12},{12,8},{1,5},{5,1},{9,13},{13,9},{2,6},{6,2},{1... | collective-permute-start | bytes 221192 | tf_op jit(solution)/shard_map/ppermute | solution.py:88
  98.3 5.2 %collective-permute-start.8 = (bf16[4,3,12,256]{3,0,2,1:T(4,128)(2,1)S(1)}, bf16[4,3,12,256]{3,0,2,1:T(4,128)(2,1)S(1)}, u32[]{:S(2)}, u32[]{:S(2)}) collective-permute-start(bf16[4,3,12,256]{3,0,2,1:T(4,128)(2,1)S(1)} %get-tuple-element.21), channel_id=1, source_target_pairs={{0,8},{4,12},{8,0},{12,4},{1,9},{5,13},{9,1},{13,5},{2,10},{6,14},... | collective-permute-start | bytes 221192 | tf_op jit(solution)/shard_map/ppermute | solution.py:88
  98.7 5.2 %collective-permute-start.9 = (bf16[4,3,12,256]{3,0,2,1:T(4,128)(2,1)S(1)}, bf16[4,3,12,256]{3,0,2,1:T(4,128)(2,1)S(1)}, u32[]{:S(2)}, u32[]{:S(2)}) collective-permute-start(bf16[4,3,12,256]{3,0,2,1:T(4,128)(2,1)S(1)} %get-tuple-element.20), channel_id=1, source_target_pairs={{0,12},{4,8},{8,4},{12,0},{1,13},{5,9},{9,5},{13,1},{2,14},{6,10},... | collective-permute-start | bytes 221192 | tf_op jit(solution)/shard_map/ppermute | solution.py:88
  (5 other events, 4.8 us)
